TPU v7x, 128 devices: a whole 4x4x4 slice. The times are simulated.
128 devices in a mesh: group: 8 (over y, core), member: 16 (over z, x).
Axes of the slice: x: 4, y: 4, z: 4, core: 2. Of those that a mesh axis runs over, the one named last changes fastest.
Arguments:
- candidates: bfloat16 [512, 64, 1024], P('member', 'group'), may hold values from -6 to 6
- kv_cache: bfloat16 [64, 2048, 2048], P('group', 'member'), may hold values from -6 to 6
- cache_request: int32 [64], replicated, may hold values from 0 to 63, as said below
- rank_request: int32 [64], replicated, may hold values from 0 to 63, as said below
- hist_blocks: int32 [64], replicated, may hold values from 1 to 16, 544 in all
- w_uq: bfloat16 [1024, 2048], replicated, may hold values from -0.1875 to 0.1875
- w_out: bfloat16 [1024, 1024], replicated, may hold values from -0.1875 to 0.1875
Outputs:
- ranked: bfloat16 [512, 64, 1024], P('member', 'group')
Inputs may be any that keep to these rules, and one draw needn't show every extreme that they name: `cache_request`: A permutation; cache row q lies on group q // 8, events split over member. `rank_request`: A permutation; group g ranks positions g * 8 to (g + 1) * 8 - 1. The requests cached on one group are dealt out to the ranking groups in turn, so every pair of groups carries 8 // 8 or 1 requests and some pair carries exactly 1; the uneven part of the load is the live history lengths.
All inputs are finite; a program needn't handle non-finite values.
Results may differ from a plain program's by a relative error of at most 0.011.
Values may be sent and summed in bfloat16 or wider, within the bound.
No kernel may reach another device: no remote copies, remote signals or barrier semaphores. Data moves between devices by JAX's collectives and lax.ppermute only.
A program may use at most 320 MiB of HBM per device.

v0:
```python
import jax
import jax.numpy as jnp
from jax import lax
from jax.sharding import PartitionSpec as P

HEADS = 8
BLK = 128


def layer_norm(values):
    center = values - jnp.mean(values, axis=-1, keepdims=True)
    spread = jnp.mean(center * center, axis=-1, keepdims=True)
    return center * lax.rsqrt(spread + 1e-05)


def routing(cache_request, rank_request, per_group):
    slot_ids = jnp.arange(cache_request.shape[0], dtype=jnp.int32)
    match = cache_request[:, None] == rank_request[None, :]
    rank_pos = jnp.sum(jnp.where(match, slot_ids[None, :], 0), axis=1)
    target = rank_pos // per_group
    owner_grp = slot_ids // per_group
    earlier = (
        (owner_grp[:, None] == owner_grp[None, :])
        & (target[:, None] == target[None, :])
        & (slot_ids[None, :] < slot_ids[:, None])
    )
    arrival = jnp.sum(earlier.astype(jnp.int32), axis=1)
    slot_of_pos = jnp.sum(jnp.where(match, slot_ids[:, None], 0), axis=0)
    return (target, arrival, slot_of_pos)


def attend_local(queries, piece, live, first_event, scale):
    rows, count = (piece.shape[0], piece.shape[1])
    heads, head_dim = (queries.shape[2], queries.shape[3])
    width = heads * head_dim
    keys = piece[:, :, :width].reshape(rows, count, heads, head_dim)
    values = piece[:, :, width:].reshape(rows, count, heads, head_dim)
    scores = jnp.einsum("rchd,rehd->rhce", queries, keys, preferred_element_type=jnp.float32)
    events = (first_event + jnp.arange(count)).astype(jnp.float32)
    keep = (events[None, :] < live[:, None]).astype(jnp.float32) / live[:, None]
    weights = (jax.nn.silu(scores * scale) * keep[:, None, None, :]).astype(jnp.bfloat16)
    return jnp.einsum("rhce,rehd->rchd", weights, values, preferred_element_type=jnp.float32)


def on_device(candidates, kv_cache, cache_request, rank_request, hist_blocks, w_uq, w_out):
    groups = lax.axis_size("group")
    per_group = kv_cache.shape[0]
    cand_rows = candidates.shape[0]
    width = candidates.shape[2]
    head_dim = width // HEADS
    count = kv_cache.shape[1]
    capacity = (per_group + groups - 1) // groups
    group_now = lax.axis_index("group")
    member_now = lax.axis_index("member")
    target, arrival, slot_of_pos = routing(cache_request, rank_request, per_group)
    first_slot = group_now * per_group
    local_target = lax.dynamic_slice_in_dim(target, first_slot, per_group)
    local_arrival = lax.dynamic_slice_in_dim(arrival, first_slot, per_group)
    row_index = local_target * capacity + local_arrival
    target_grid = jnp.arange(groups)[:, None, None]
    place_grid = jnp.arange(capacity)[None, :, None]
    hits = (local_target[None, None, :] == target_grid) & (
        local_arrival[None, None, :] == place_grid
    )
    chosen = jnp.sum(jnp.where(hits, jnp.arange(per_group)[None, None, :], 0), axis=2).reshape(-1)
    filled = jnp.any(hits, axis=2).reshape(-1)
    positions = first_slot + jnp.arange(per_group)
    source_slot = slot_of_pos[positions]
    receive_index = source_slot // per_group * capacity + arrival[source_slot]
    send_hits = receive_index[None, :] == jnp.arange(groups * capacity)[:, None]
    send_pos = jnp.sum(jnp.where(send_hits, jnp.arange(per_group)[None, :], 0), axis=1)
    send_filled = jnp.any(send_hits, axis=1)
    row_live = (hist_blocks[cache_request[first_slot + jnp.arange(per_group)]] * BLK).astype(
        jnp.float32
    )
    inputs = candidates.astype(jnp.float32)
    normed = layer_norm(inputs).astype(jnp.bfloat16).reshape(cand_rows * per_group, width)
    projected = jax.nn.silu(jnp.dot(normed, w_uq, preferred_element_type=jnp.float32))
    gates = projected[:, :width].reshape(cand_rows, per_group, width)
    queries = projected[:, width:].astype(jnp.bfloat16).reshape(cand_rows, per_group, width)
    scale = head_dim ** (-0.5)
    q_pos = jnp.swapaxes(queries, 0, 1)
    q_out = jnp.where(send_filled[:, None, None], q_pos[send_pos], jnp.zeros((), jnp.bfloat16))
    q_in = lax.all_to_all(q_out, "group", split_axis=0, concat_axis=0, tiled=True)
    q_rows = q_in[row_index]
    q_all = lax.all_gather(q_rows, "member", axis=1, tiled=True)
    q_all = q_all.reshape(per_group, q_all.shape[1], HEADS, head_dim)
    partial = attend_local(q_all, kv_cache, row_live, member_now * count, scale)
    partial = partial.reshape(per_group, partial.shape[1], width)
    summed = lax.psum_scatter(partial, "member", scatter_dimension=1, tiled=True)
    a_out = jnp.where(filled[:, None, None], summed[chosen], jnp.zeros((), jnp.float32))
    a_in = lax.all_to_all(a_out, "group", split_axis=0, concat_axis=0, tiled=True)
    attn = jnp.swapaxes(a_in[receive_index], 0, 1)
    gated = (layer_norm(attn) * gates).astype(jnp.bfloat16).reshape(cand_rows * per_group, width)
    result = jnp.dot(gated, w_out, preferred_element_type=jnp.float32) + inputs.reshape(
        cand_rows * per_group, width
    )
    return result.astype(jnp.bfloat16).reshape(cand_rows, per_group, width)


def solution(mesh):
    return jax.shard_map(
        on_device,
        mesh=mesh,
        in_specs=(P("member", "group", None), P("group", "member", None), P(), P(), P(), P(), P()),
        out_specs=P("member", "group", None),
        check_vma=False,
    )
```

profile of v0, /device:TPU:1, one launch (start us, length us, event | category | flops | bytes accessed | tf_op | source)
XLA Modules:
  0.0 296.7 jit_solution(6112455092179821543)
XLA Ops:
  6.5 1.0 fusion.19
  9.3 1.2 convert_reduce_fusion
  10.7 1.3 fusion.5
  12.2 3.8 %divide_multiply_fusion = f32[256,2048]{1,0:T(8,128)S(1)} fusion(bf16[1024,2048]{1,0:T(8,128)(2,1)} %param.12, bf16[32,8,1024]{2,1,0:T(8,128)(2,1)} %param.7, f32[32,8]{1,0:T(8,128)S(1)} %copy.69, f32[32,8]{1,0:T(8,128)S(1)} %copy.67), kind=kOutput, calls=%fused_computation.10 | convolution fusion | flops 1076887552 | bytes 6817792 | tf_op jit(solution)/shard_map/dot_general | solution.py:78
  17.9 0.9 broadcast_select_fusion.1
  18.8 6.0 %all-to-all-start = ((bf16[8,32,1024]{2,1,0:T(8,128)(2,1)}), bf16[8,32,1024]{2,1,0:T(8,128)(2,1)S(1)}, u32[]{:S(2)}, u32[]{:S(2)}) async-start(bf16[8,32,1024]{2,1,0:T(8,128)(2,1)} %broadcast_select_fusion.1), calls=%async_computation | async-start | bytes 1048576 | tf_op jit(solution)/shard_map/all_to_all | solution.py:84
  24.9 9.3 %all-to-all-done = bf16[8,32,1024]{2,1,0:T(8,128)(2,1)S(1)} async-done(((bf16[8,32,1024]{2,1,0:T(8,128)(2,1)}), bf16[8,32,1024]{2,1,0:T(8,128)(2,1)S(1)}, u32[]{:S(2)}, u32[]{:S(2)}) %all-to-all-start) | async-done | bytes 524320 | tf_op jit(solution)/shard_map/all_to_all | solution.py:84
  34.1 1.4 gather_fusion.3
  36.2 4.9 %fusion.33 = (bf16[8,128,1024]{2,1,0:T(8,128)(2,1)}, bf16[8,128,1024]{2,1,0:T(8,128)(2,1)}) fusion(bf16[8,128,2048]{2,1,0:T(8,128)(2,1)} %param.8), kind=kLoop, calls=%fused_computation.101 | loop fusion | bytes 8388608 | tf_op jit(solution)/shard_map/slice | solution.py:36
  41.1 3.9 %copy.75 = bf16[8,128,1024]{1,2,0:T(8,128)(2,1)} copy(bf16[8,128,1024]{2,1,0:T(8,128)(2,1)} %get-tuple-element.10) | data formatting | bytes 4194304 | tf_op jit(solution)/shard_map/slice | solution.py:37
  45.0 4.0 %copy.81 = bf16[8,128,1024]{1,2,0:T(8,128)(2,1)} copy(bf16[8,128,1024]{2,1,0:T(8,128)(2,1)} %get-tuple-element.9) | data formatting | bytes 4194304
  49.8 57.3 %all-gather.3.cloned.1.call-done = bf16[8,512,1024]{2,1,0:T(8,128)(2,1)} async-done(((bf16[8,32,1024]{2,1,0:T(8,128)(2,1)}), bf16[8,512,1024]{2,1,0:T(8,128)(2,1)}) %all-gather.3.cloned.1.call-update) | async-done | bytes 8388624 | tf_op jit(solution)/shard_map/all_gather | solution.py:86
  107.1 11.4 %copy.71 = bf16[8,512,1024]{1,2,0:T(8,128)(2,1)} copy(bf16[8,512,1024]{2,1,0:T(8,128)(2,1)} %all-gather.3.cloned.1.call-done) | data formatting | bytes 16777216 | tf_op jit(solution)/shard_map/all_gather | solution.py:86
  118.5 15.3 %fusion = f32[8,8,512,128]{2,3,1,0:T(8,128)} fusion(bf16[8,128,8,128]{1,3,2,0:T(8,128)(2,1)} %bitcast.74, bf16[8,512,8,128]{1,3,2,0:T(8,128)(2,1)} %bitcast.73, bf16[8,128,8,128]{1,3,2,0:T(8,128)(2,1)} %bitcast.75, f32[8,128]{1,0:T(8,128)S(1)} %convert_divide_fusion), kind=kOutput, calls=%fused_computation.9 | convolution fusion | flops 2176843776 | bytes 29364224 | tf_op jit(solution)/shard_map/rhce,rehd->rchd/dot_general | solution.py:42
  133.8 16.4 %copy.76 = f32[8,512,1024]{2,1,0:T(8,128)} copy(f32[8,512,1024]{1,2,0:T(8,128)} %bitcast.72) | data formatting | bytes 33554432 | tf_op jit(solution)/shard_map/reshape | solution.py:89
  150.5 110.2 %reduce-scatter.2.cloned.1.call-done = f32[8,32,1024]{2,1,0:T(8,128)} async-done(((f32[8,512,1024]{2,1,0:T(8,128)}), f32[8,32,1024]{2,1,0:T(8,128)}) %reduce-scatter.2.cloned.1.call-update) | async-done | bytes 1048592 | tf_op jit(solution)/shard_map/reduce_scatter | solution.py:90
  260.7 1.8 gather_fusion.6
  262.6 1.2 broadcast_select_fusion
  263.7 5.2 %all-to-all-start.1 = ((f32[8,32,1024]{2,1,0:T(8,128)}), f32[8,32,1024]{2,1,0:T(8,128)}, u32[]{:S(2)}, u32[]{:S(2)}) async-start(f32[8,32,1024]{2,1,0:T(8,128)} %broadcast_select_fusion), calls=%async_computation.2 | async-start | bytes 2097152 | tf_op jit(solution)/shard_map/all_to_all | solution.py:92
  269.0 2.4 slice_bitcast_fusion
  271.3 12.7 %all-to-all-done.1 = f32[8,32,1024]{2,1,0:T(8,128)} async-done(((f32[8,32,1024]{2,1,0:T(8,128)}), f32[8,32,1024]{2,1,0:T(8,128)}, u32[]{:S(2)}, u32[]{:S(2)}) %all-to-all-start.1) | async-done | bytes 1048608 | tf_op jit(solution)/shard_map/all_to_all | solution.py:92
  284.0 1.8 gather_fusion.7
  286.3 1.9 fusion.7
  288.2 1.6 fusion.4
  (56 shorter events, 6.2 us)
Async XLA Ops:
  6.5 281.6 %copy-start = (bf16[1024,1024]{1,0:T(8,128)(2,1)S(1)}, bf16[1024,1024]{1,0:T(8,128)(2,1)}, u32[]{:S(2)}) copy-start(bf16[1024,1024]{1,0:T(8,128)(2,1)} %param.13) | copy-start | bytes 6291460
  16.0 1.3 copy-start.4
  16.0 19.6 %copy-start.1 = (s32[64]{0:T(128)S(1)}, s32[64]{0:T(128)}, u32[]{:S(2)}) copy-start(s32[64]{0:T(128)} %param.9) | copy-start | bytes 772
  18.8 15.3 %all-to-all-start = ((bf16[8,32,1024]{2,1,0:T(8,128)(2,1)}), bf16[8,32,1024]{2,1,0:T(8,128)(2,1)S(1)}, u32[]{:S(2)}, u32[]{:S(2)}) async-start(bf16[8,32,1024]{2,1,0:T(8,128)(2,1)} %broadcast_select_fusion.1), calls=%async_computation | async-start | bytes 1048576 | tf_op jit(solution)/shard_map/all_to_all | solution.py:84
  24.8 82.3 %all-gather.3.cloned.1.call-start = ((), (), s32[]{:S(2)}) async-start(), calls=%async_computation.4 | async-start | bytes 8912896 | tf_op jit(solution)/shard_map/all_gather | solution.py:86
  35.5 225.2 %reduce-scatter.2.cloned.1.call-start = ((), (), s32[]{:S(2)}) async-start(), calls=%async_computation.3 | async-start | bytes 17825792 | tf_op jit(solution)/shard_map/reduce_scatter | solution.py:90
  41.1 7.9 %copy-start.2 = (s32[64]{0:T(128)S(1)}, s32[64]{0:T(128)}, u32[]{:S(2)}) copy-start(s32[64]{0:T(128)} %param.11) | copy-start | bytes 772
  263.7 20.3 %all-to-all-start.1 = ((f32[8,32,1024]{2,1,0:T(8,128)}), f32[8,32,1024]{2,1,0:T(8,128)}, u32[]{:S(2)}, u32[]{:S(2)}) async-start(f32[8,32,1024]{2,1,0:T(8,128)} %broadcast_select_fusion), calls=%async_computation.2 | async-start | bytes 2097152 | tf_op jit(solution)/shard_map/all_to_all | solution.py:92
  285.9 2.3 copy-start.3
Sparse Core Ops, SparseCore 0:
  35.6 71.4 all-gather.2
  150.3 110.3 reduce-scatter.1
where the time goes:
time: 298 us; the launch traced here: 297 us
  waiting for transfers between devices  189 us (63%)
  local copies, waits for them, and re-layouts  52.7 us (18%)
  matrix products  20.7 us (7%)
  between operations  13.6 us (5%)
  starting transfers between devices  11.2 us (4%)
  other arithmetic  8.88 us (3%)
    reduce_scatter x1, waiting for transfers between devices, on_device(): lax.psum_scatter(partial, 'member', scatter_dimension=1, tiled=True)  110 us
    all_gather x1, waiting for transfers between devices, on_device(): q_all = lax.all_gather(q_rows, 'member', axis=1, tiled=True)  57.3 us
    reshape x1, local copies, waits for them, and re-layouts, on_device(): partial = partial.reshape(per_group, partial.shape[1], width)  16.4 us
    dot_general x1, matrix products, attend_local(): jnp.einsum('rhce,rehd->rchd', weights, values, preferred_element_type=jnp...  15.3 us
    all_to_all x1, waiting for transfers between devices, on_device(): lax.all_to_all(a_out, 'group', split_axis=0, concat_axis=0, tiled=True)  12.7 us
    all_gather x1, local copies, waits for them, and re-layouts, on_device(): q_all = lax.all_gather(q_rows, 'member', axis=1, tiled=True)  11.4 us
    all_to_all x1, waiting for transfers between devices, on_device(): lax.all_to_all(q_out, 'group', split_axis=0, concat_axis=0, tiled=True)  9.26 us
  transfers between devices with their start and end apart: 4, of which 4 were waited for; matrix products, arithmetic and copies ran while one was open for 6% of the time, Pallas kernels for 0%

commit v1 on v0

--- a/solution.py
+++ b/solution.py
@@ -83,7 +83,24 @@
     q_out = jnp.where(send_filled[:, None, None], q_pos[send_pos], jnp.zeros((), jnp.bfloat16))
     q_in = lax.all_to_all(q_out, "group", split_axis=0, concat_axis=0, tiled=True)
     q_rows = q_in[row_index]
-    q_all = lax.all_gather(q_rows, "member", axis=1, tiled=True)
+    devices, index, span = (lax.axis_size("member"), lax.axis_index("member"), q_rows.shape[1])
+    right = [(i, (i + 1) % devices) for i in range(devices)]
+    downward = [(i, (i - 1) % devices) for i in range(devices)]
+    result_2 = jnp.zeros((*q_rows.shape[:1], devices * span, *q_rows.shape[1 + 1 :]), q_rows.dtype)
+    result_2 = lax.dynamic_update_slice_in_dim(result_2, q_rows, index * span, axis=1)
+    from_left = from_right = q_rows
+    half = devices // 2
+    for step in range(1, half + 1):
+        from_left = lax.ppermute(from_left, "member", right)
+        result_2 = lax.dynamic_update_slice_in_dim(
+            result_2, from_left, (index - step) % devices * span, axis=1
+        )
+        if step < devices - half:
+            from_right = lax.ppermute(from_right, "member", downward)
+            result_2 = lax.dynamic_update_slice_in_dim(
+                result_2, from_right, (index + step) % devices * span, axis=1
+            )
+    q_all = result_2
     q_all = q_all.reshape(per_group, q_all.shape[1], HEADS, head_dim)
     partial = attend_local(q_all, kv_cache, row_live, member_now * count, scale)
     partial = partial.reshape(per_group, partial.shape[1], width)

time: 298 us -> 735 us (2.47); the launches traced: 297 us -> 725 us
  local copies, waits for them, and re-layouts: 52.7 us -> 442 us
  starting transfers between devices: 11.2 us -> 46.1 us
    dynamic_update_slice x0 -> x16, local copies, waits for them, and re-layouts: none -> 364 us  [the longest x8 180 us: on_device(): lax.dynamic_update_slice_in_dim(result_2, from_left, (index - step) % dev...]
    all_gather x1 -> x0, waiting for transfers between devices: 57.3 us -> none  [on_device(): q_all = lax.all_gather(q_rows, 'member', axis=1, tiled=True)]
    ppermute x0 -> x15, waiting for transfers between devices: none -> 55.1 us  [the longest x8 55.1 us: on_device(): from_left = lax.ppermute(from_left, 'member', right)]
    ppermute x0 -> x15, starting transfers between devices: none -> 34.9 us  [the longest x7 33.5 us: on_device(): from_right = lax.ppermute(from_right, 'member', downward)]
    ppermute x0 -> x15, local copies, waits for them, and re-layouts: none -> 31.2 us  [the longest x8 16.5 us: on_device(): from_left = lax.ppermute(from_left, 'member', right)]
    all_gather x1 -> x0, local copies, waits for them, and re-layouts: 11.4 us -> none  [on_device(): q_all = lax.all_gather(q_rows, 'member', axis=1, tiled=True)]
  transfers between devices with their start and end apart: 4 -> 18, of which waited for: 4 -> 9; matrix products, arithmetic and copies ran while one was open for 6% -> 54% of each run, Pallas kernels for 0% -> 0%
where the time goes in v1:
time: 735 us; the launch traced here: 725 us
  local copies, waits for them, and re-layouts  442 us (60%)
  waiting for transfers between devices  194 us (26%)
  starting transfers between devices  46.1 us (6%)
  matrix products  20.7 us (3%)
  between operations  13.8 us (2%)
  other arithmetic  8.86 us (1%)
    dynamic_update_slice x8, local copies, waits for them, and re-layouts, on_device(): lax.dynamic_update_slice_in_dim(result_2, from_left, (index - step) % dev...  180 us
    dynamic_update_slice x7, local copies, waits for them, and re-layouts, on_device(): lax.dynamic_update_slice_in_dim(result_2, from_right, (index + step) % de...  163 us
    reduce_scatter x1, waiting for transfers between devices, on_device(): lax.psum_scatter(partial, 'member', scatter_dimension=1, tiled=True)  117 us
    ppermute x8, waiting for transfers between devices, on_device(): from_left = lax.ppermute(from_left, 'member', right)  55.1 us
    ppermute x7, starting transfers between devices, on_device(): from_right = lax.ppermute(from_right, 'member', downward)  33.5 us
    dynamic_update_slice x1, local copies, waits for them, and re-layouts, on_device(): lax.dynamic_update_slice_in_dim(result_2, q_rows, index * span, axis=1)  20.5 us
    ppermute x8, local copies, waits for them, and re-layouts, on_device(): from_left = lax.ppermute(from_left, 'member', right)  16.5 us
    reshape x1, local copies, waits for them, and re-layouts, on_device(): partial = partial.reshape(per_group, partial.shape[1], width)  16.4 us
  transfers between devices with their start and end apart: 18, of which 9 were waited for; matrix products, arithmetic and copies ran while one was open for 54% of the time, Pallas kernels for 0%

profile of v1, /device:TPU:1, one launch (start us, length us, event | category | flops | bytes accessed | tf_op | source)
XLA Modules:
  0.0 725.0 jit_solution(16052318051658382764)
XLA Ops:
  24.9 9.3 %all-to-all-done = bf16[8,32,1024]{2,1,0:T(8,128)(2,1)S(1)} async-done(((bf16[8,32,1024]{2,1,0:T(8,128)(2,1)}), bf16[8,32,1024]{2,1,0:T(8,128)(2,1)S(1)}, u32[]{:S(2)}, u32[]{:S(2)}) %all-to-all-start) | async-done | bytes 524320 | tf_op jit(solution)/shard_map/all_to_all | solution.py:84
  40.8 11.2 %collective-permute-done = bf16[8,32,1024]{2,1,0:T(8,128)(2,1)S(1)} collective-permute-done((bf16[8,32,1024]{2,1,0:T(8,128)(2,1)S(1)}, bf16[8,32,1024]{2,1,0:T(8,128)(2,1)S(1)}, u32[]{:S(2)}, u32[]{:S(2)}) %collective-permute-start) | collective-permute-done | bytes 524320 | tf_op jit(solution)/shard_map/ppermute | solution.py:94
  56.9 10.5 %collective-permute-done.2 = bf16[8,32,1024]{2,1,0:T(8,128)(2,1)S(1)} collective-permute-done((bf16[8,32,1024]{2,1,0:T(8,128)(2,1)S(1)}, bf16[8,32,1024]{2,1,0:T(8,128)(2,1)S(1)}, u32[]{:S(2)}, u32[]{:S(2)}) %collective-permute-start.2) | collective-permute-done | bytes 524320 | tf_op jit(solution)/shard_map/ppermute | solution.py:94
  72.1 9.6 %collective-permute-done.4 = bf16[8,32,1024]{2,1,0:T(8,128)(2,1)S(1)} collective-permute-done((bf16[8,32,1024]{2,1,0:T(8,128)(2,1)S(1)}, bf16[8,32,1024]{2,1,0:T(8,128)(2,1)S(1)}, u32[]{:S(2)}, u32[]{:S(2)}) %collective-permute-start.4) | collective-permute-done | bytes 524320 | tf_op jit(solution)/shard_map/ppermute | solution.py:94
  144.7 20.5 %dynamic_update_slice.48 = bf16[8,512,1024]{1,2,0:T(8,128)(2,1)} dynamic-update-slice(bf16[8,512,1024]{1,2,0:T(8,128)(2,1)} %broadcast_in_dim.74, bf16[8,32,1024]{1,2,0:T(8,128)(2,1)} %copy.146, s32[]{:T(128)} %constant.143.clone.1, s32[]{:T(128)S(6)} %select_n.265, s32[]{:T(128)} %constant.143.clone.1) | dynamic-update-slice | bytes 1048580 | tf_op jit(solution)/shard_map/dynamic_update_slice | solution.py:90
  167.8 22.9 %dynamic_update_slice.49 = bf16[8,512,1024]{1,2,0:T(8,128)(2,1)} dynamic-update-slice(bf16[8,512,1024]{1,2,0:T(8,128)(2,1)} %dynamic_update_slice.48, bf16[8,32,1024]{1,2,0:T(8,128)(2,1)} %copy.147, s32[]{:T(128)} %constant.143.clone.1, s32[]{:T(128)S(6)} %select_n.267, s32[]{:T(128)} %constant.143.clone.1) | dynamic-update-slice | bytes 1048580 | tf_op jit(solution)/shard_map/dynamic_update_slice | solution.py:95
  192.5 23.8 %dynamic_update_slice.50 = bf16[8,512,1024]{1,2,0:T(8,128)(2,1)} dynamic-update-slice(bf16[8,512,1024]{1,2,0:T(8,128)(2,1)} %dynamic_update_slice.49, bf16[8,32,1024]{1,2,0:T(8,128)(2,1)} %copy.148, s32[]{:T(128)} %constant.143.clone.1, s32[]{:T(128)S(6)} %select_n.269, s32[]{:T(128)} %constant.143.clone.1) | dynamic-update-slice | bytes 1048580 | tf_op jit(solution)/shard_map/dynamic_update_slice | solution.py:100
  218.0 23.0 %dynamic_update_slice.51 = bf16[8,512,1024]{1,2,0:T(8,128)(2,1)} dynamic-update-slice(bf16[8,512,1024]{1,2,0:T(8,128)(2,1)} %dynamic_update_slice.50, bf16[8,32,1024]{1,2,0:T(8,128)(2,1)} %copy.149, s32[]{:T(128)} %constant.143.clone.1, s32[]{:T(128)S(6)} %select_n.271, s32[]{:T(128)} %constant.143.clone.1) | dynamic-update-slice | bytes 1048580 | tf_op jit(solution)/shard_map/dynamic_update_slice | solution.py:95
  242.8 23.8 %dynamic_update_slice.52 = bf16[8,512,1024]{1,2,0:T(8,128)(2,1)} dynamic-update-slice(bf16[8,512,1024]{1,2,0:T(8,128)(2,1)} %dynamic_update_slice.51, bf16[8,32,1024]{1,2,0:T(8,128)(2,1)} %copy.150, s32[]{:T(128)} %constant.143.clone.1, s32[]{:T(128)S(6)} %select_n.273, s32[]{:T(128)} %constant.143.clone.1) | dynamic-update-slice | bytes 1048580 | tf_op jit(solution)/shard_map/dynamic_update_slice | solution.py:100
  268.3 23.0 %dynamic_update_slice.53 = bf16[8,512,1024]{1,2,0:T(8,128)(2,1)} dynamic-update-slice(bf16[8,512,1024]{1,2,0:T(8,128)(2,1)} %dynamic_update_slice.52, bf16[8,32,1024]{1,2,0:T(8,128)(2,1)} %copy.151, s32[]{:T(128)} %constant.143.clone.1, s32[]{:T(128)S(6)} %select_n.275, s32[]{:T(128)} %constant.143.clone.1) | dynamic-update-slice | bytes 1048580 | tf_op jit(solution)/shard_map/dynamic_update_slice | solution.py:95
  293.1 23.8 %dynamic_update_slice.54 = bf16[8,512,1024]{1,2,0:T(8,128)(2,1)} dynamic-update-slice(bf16[8,512,1024]{1,2,0:T(8,128)(2,1)} %dynamic_update_slice.53, bf16[8,32,1024]{1,2,0:T(8,128)(2,1)} %copy.152, s32[]{:T(128)} %constant.143.clone.1, s32[]{:T(128)S(6)} %select_n.277, s32[]{:T(128)} %constant.143.clone.1) | dynamic-update-slice | bytes 1048580 | tf_op jit(solution)/shard_map/dynamic_update_slice | solution.py:100
  318.6 19.6 %dynamic_update_slice.55 = bf16[8,512,1024]{1,2,0:T(8,128)(2,1)} dynamic-update-slice(bf16[8,512,1024]{1,2,0:T(8,128)(2,1)} %dynamic_update_slice.54, bf16[8,32,1024]{1,2,0:T(8,128)(2,1)} %copy.153, s32[]{:T(128)} %constant.143.clone.1, s32[]{:T(128)S(6)} %select_n.279, s32[]{:T(128)} %constant.143.clone.1) | dynamic-update-slice | bytes 1048580 | tf_op jit(solution)/shard_map/dynamic_update_slice | solution.py:95
  340.0 20.5 %dynamic_update_slice.56 = bf16[8,512,1024]{1,2,0:T(8,128)(2,1)} dynamic-update-slice(bf16[8,512,1024]{1,2,0:T(8,128)(2,1)} %dynamic_update_slice.55, bf16[8,32,1024]{1,2,0:T(8,128)(2,1)} %copy.154, s32[]{:T(128)} %constant.143.clone.1, s32[]{:T(128)S(6)} %select_n.281, s32[]{:T(128)} %constant.143.clone.1) | dynamic-update-slice | bytes 1048580 | tf_op jit(solution)/shard_map/dynamic_update_slice | solution.py:100
  362.2 23.8 %dynamic_update_slice.57 = bf16[8,512,1024]{1,2,0:T(8,128)(2,1)} dynamic-update-slice(bf16[8,512,1024]{1,2,0:T(8,128)(2,1)} %dynamic_update_slice.56, bf16[8,32,1024]{1,2,0:T(8,128)(2,1)} %copy.155, s32[]{:T(128)} %constant.143.clone.1, s32[]{:T(128)S(6)} %select_n.283, s32[]{:T(128)} %constant.143.clone.1) | dynamic-update-slice | bytes 1048580 | tf_op jit(solution)/shard_map/dynamic_update_slice | solution.py:95
  388.6 23.8 %dynamic_update_slice.58 = bf16[8,512,1024]{1,2,0:T(8,128)(2,1)} dynamic-update-slice(bf16[8,512,1024]{1,2,0:T(8,128)(2,1)} %dynamic_update_slice.57, bf16[8,32,1024]{1,2,0:T(8,128)(2,1)} %copy.156, s32[]{:T(128)} %constant.143.clone.1, s32[]{:T(128)S(6)} %select_n.285, s32[]{:T(128)} %constant.143.clone.1) | dynamic-update-slice | bytes 1048580 | tf_op jit(solution)/shard_map/dynamic_update_slice | solution.py:100
  415.0 23.8 %dynamic_update_slice.59 = bf16[8,512,1024]{1,2,0:T(8,128)(2,1)} dynamic-update-slice(bf16[8,512,1024]{1,2,0:T(8,128)(2,1)} %dynamic_update_slice.58, bf16[8,32,1024]{1,2,0:T(8,128)(2,1)} %copy.157, s32[]{:T(128)} %constant.143.clone.1, s32[]{:T(128)S(6)} %select_n.287, s32[]{:T(128)} %constant.143.clone.1) | dynamic-update-slice | bytes 1048580 | tf_op jit(solution)/shard_map/dynamic_update_slice | solution.py:95
  441.3 23.8 %dynamic_update_slice.60 = bf16[8,512,1024]{1,2,0:T(8,128)(2,1)} dynamic-update-slice(bf16[8,512,1024]{1,2,0:T(8,128)(2,1)} %dynamic_update_slice.59, bf16[8,32,1024]{1,2,0:T(8,128)(2,1)} %copy.158, s32[]{:T(128)} %constant.143.clone.1, s32[]{:T(128)S(6)} %select_n.289, s32[]{:T(128)} %constant.143.clone.1) | dynamic-update-slice | bytes 1048580 | tf_op jit(solution)/shard_map/dynamic_update_slice | solution.py:100
  466.8 23.8 %dynamic_update_slice.61 = bf16[8,512,1024]{1,2,0:T(8,128)(2,1)} dynamic-update-slice(bf16[8,512,1024]{1,2,0:T(8,128)(2,1)} %dynamic_update_slice.60, bf16[8,32,1024]{1,2,0:T(8,128)(2,1)} %copy.159, s32[]{:T(128)} %constant.143.clone.1, s32[]{:T(128)S(6)} %select_n.291, s32[]{:T(128)} %constant.143.clone.1) | dynamic-update-slice | bytes 1048580 | tf_op jit(solution)/shard_map/dynamic_update_slice | solution.py:95
  493.2 23.8 %dynamic_update_slice.62 = bf16[8,512,1024]{1,2,0:T(8,128)(2,1)} dynamic-update-slice(bf16[8,512,1024]{1,2,0:T(8,128)(2,1)} %dynamic_update_slice.61, bf16[8,32,1024]{1,2,0:T(8,128)(2,1)} %copy.160, s32[]{:T(128)} %constant.143.clone.1, s32[]{:T(128)S(6)} %select_n.293, s32[]{:T(128)} %constant.143.clone.1) | dynamic-update-slice | bytes 1048580 | tf_op jit(solution)/shard_map/dynamic_update_slice | solution.py:100
  519.6 20.5 %dynamic_update_slice.63 = bf16[8,512,1024]{1,2,0:T(8,128)(2,1)} dynamic-update-slice(bf16[8,512,1024]{1,2,0:T(8,128)(2,1)} %dynamic_update_slice.62, bf16[8,32,1024]{1,2,0:T(8,128)(2,1)} %copy.161, s32[]{:T(128)} %constant.143.clone.1, s32[]{:T(128)S(6)} %select_n.295, s32[]{:T(128)} %constant.143.clone.1) | dynamic-update-slice | bytes 1048580 | tf_op jit(solution)/shard_map/dynamic_update_slice | solution.py:95
  540.1 15.3 %fusion = f32[8,8,512,128]{2,3,1,0:T(8,128)} fusion(bf16[8,128,8,128]{1,3,2,0:T(8,128)(2,1)} %bitcast.74, bf16[8,512,8,128]{1,3,2,0:T(8,128)(2,1)} %bitcast.73, bf16[8,128,8,128]{1,3,2,0:T(8,128)(2,1)} %bitcast.75, f32[8,128]{1,0:T(8,128)S(1)} %convert_divide_fusion), kind=kOutput, calls=%fused_computation.9 | convolution fusion | flops 2176843776 | bytes 29364224 | tf_op jit(solution)/shard_map/rhce,rehd->rchd/dot_general | solution.py:42
  555.3 16.4 %copy.166 = f32[8,512,1024]{2,1,0:T(8,128)} copy(f32[8,512,1024]{1,2,0:T(8,128)} %bitcast.72) | data formatting | bytes 33554432 | tf_op jit(solution)/shard_map/reshape | solution.py:106
  572.1 116.9 %reduce-scatter.2.cloned.1.call-done = f32[8,32,1024]{2,1,0:T(8,128)} async-done(((f32[8,512,1024]{2,1,0:T(8,128)}), f32[8,32,1024]{2,1,0:T(8,128)}) %reduce-scatter.2.cloned.1.call-update) | async-done | bytes 1048592 | tf_op jit(solution)/shard_map/reduce_scatter | solution.py:107
  699.6 12.7 %all-to-all-done.1 = f32[8,32,1024]{2,1,0:T(8,128)} async-done(((f32[8,32,1024]{2,1,0:T(8,128)}), f32[8,32,1024]{2,1,0:T(8,128)}, u32[]{:S(2)}, u32[]{:S(2)}) %all-to-all-start.1) | async-done | bytes 1048608 | tf_op jit(solution)/shard_map/all_to_all | solution.py:109
  (149 shorter events, 145.3 us)
Async XLA Ops:
  6.5 710.0 %copy-start = (bf16[1024,1024]{1,0:T(8,128)(2,1)S(1)}, bf16[1024,1024]{1,0:T(8,128)(2,1)}, u32[]{:S(2)}) copy-start(bf16[1024,1024]{1,0:T(8,128)(2,1)} %param.13) | copy-start | bytes 6291460
  18.8 15.3 %all-to-all-start = ((bf16[8,32,1024]{2,1,0:T(8,128)(2,1)}), bf16[8,32,1024]{2,1,0:T(8,128)(2,1)S(1)}, u32[]{:S(2)}, u32[]{:S(2)}) async-start(bf16[8,32,1024]{2,1,0:T(8,128)(2,1)} %broadcast_select_fusion.1), calls=%async_computation | async-start | bytes 1048576 | tf_op jit(solution)/shard_map/all_to_all | solution.py:84
  24.8 664.2 %reduce-scatter.2.cloned.1.call-start = ((), (), s32[]{:S(2)}) async-start(), calls=%async_computation.3 | async-start | bytes 17825792 | tf_op jit(solution)/shard_map/reduce_scatter | solution.py:107
  34.7 90.2 %copy-start.1 = (s32[64]{0:T(128)S(1)}, s32[64]{0:T(128)}, u32[]{:S(2)}) copy-start(s32[64]{0:T(128)} %param.9) | copy-start | bytes 772
  34.7 17.4 %collective-permute-start = (bf16[8,32,1024]{2,1,0:T(8,128)(2,1)S(1)}, bf16[8,32,1024]{2,1,0:T(8,128)(2,1)S(1)}, u32[]{:S(2)}, u32[]{:S(2)}) collective-permute-start(bf16[8,32,1024]{2,1,0:T(8,128)(2,1)S(1)} %gather_fusion.3), channel_id=1, source_target_pairs={{0,1},{1,2},{2,3},{3,4},{4,5},{5,6},{6,7},{7,8},{8,9},{9,10},{10,1... | collective-permute-start | bytes 1572872 | tf_op jit(solution)/shard_map/ppermute | solution.py:94
  36.0 16.1 %collective-permute-start.1 = (bf16[8,32,1024]{2,1,0:T(8,128)(2,1)S(1)}, bf16[8,32,1024]{2,1,0:T(8,128)(2,1)S(1)}, u32[]{:S(2)}, u32[]{:S(2)}) collective-permute-start(bf16[8,32,1024]{2,1,0:T(8,128)(2,1)S(1)} %gather_fusion.3), channel_id=1, source_target_pairs={{0,15},{1,0},{2,1},{3,2},{4,3},{5,4},{6,5},{7,6},{8,7},{9,8},{10,9... | collective-permute-start | bytes 1572872 | tf_op jit(solution)/shard_map/ppermute | solution.py:99
  52.1 67.8 %copy-start.9 = (bf16[8,32,1024]{2,1,0:T(8,128)(2,1)}, bf16[8,32,1024]{2,1,0:T(8,128)(2,1)S(1)}, u32[]{:S(2)}) copy-start(bf16[8,32,1024]{2,1,0:T(8,128)(2,1)S(1)} %collective-permute-done) | copy-start | bytes 1572868
  52.1 15.3 %collective-permute-start.2 = (bf16[8,32,1024]{2,1,0:T(8,128)(2,1)S(1)}, bf16[8,32,1024]{2,1,0:T(8,128)(2,1)S(1)}, u32[]{:S(2)}, u32[]{:S(2)}) collective-permute-start(bf16[8,32,1024]{2,1,0:T(8,128)(2,1)S(1)} %collective-permute-done), channel_id=1, source_target_pairs={{0,1},{1,2},{2,3},{3,4},{4,5},{5,6},{6,7},{7,8},{8,9},{9,10},{10,1... | collective-permute-start | bytes 1572872 | tf_op jit(solution)/shard_map/ppermute | solution.py:94
  52.1 60.7 %copy-start.5 = (bf16[8,32,1024]{2,1,0:T(8,128)(2,1)}, bf16[8,32,1024]{2,1,0:T(8,128)(2,1)S(1)}, u32[]{:S(2)}) copy-start(bf16[8,32,1024]{2,1,0:T(8,128)(2,1)S(1)} %collective-permute-done.1) | copy-start | bytes 1572868
  52.1 15.2 %collective-permute-start.3 = (bf16[8,32,1024]{2,1,0:T(8,128)(2,1)S(1)}, bf16[8,32,1024]{2,1,0:T(8,128)(2,1)S(1)}, u32[]{:S(2)}, u32[]{:S(2)}) collective-permute-start(bf16[8,32,1024]{2,1,0:T(8,128)(2,1)S(1)} %collective-permute-done.1), channel_id=1, source_target_pairs={{0,15},{1,0},{2,1},{3,2},{4,3},{5,4},{6,5},{7,6},{8,7},{9,8},{10,9... | collective-permute-start | bytes 1572872 | tf_op jit(solution)/shard_map/ppermute | solution.py:99
  67.3 52.6 %copy-start.7 = (bf16[8,32,1024]{2,1,0:T(8,128)(2,1)}, bf16[8,32,1024]{2,1,0:T(8,128)(2,1)S(1)}, u32[]{:S(2)}) copy-start(bf16[8,32,1024]{2,1,0:T(8,128)(2,1)S(1)} %collective-permute-done.2) | copy-start | bytes 1572868
  67.3 14.4 %collective-permute-start.4 = (bf16[8,32,1024]{2,1,0:T(8,128)(2,1)S(1)}, bf16[8,32,1024]{2,1,0:T(8,128)(2,1)S(1)}, u32[]{:S(2)}, u32[]{:S(2)}) collective-permute-start(bf16[8,32,1024]{2,1,0:T(8,128)(2,1)S(1)} %collective-permute-done.2), channel_id=1, source_target_pairs={{0,1},{1,2},{2,3},{3,4},{4,5},{5,6},{6,7},{7,8},{8,9},{9,10},{10,1... | collective-permute-start | bytes 1572872 | tf_op jit(solution)/shard_map/ppermute | solution.py:94
  67.3 52.6 %copy-start.10 = (bf16[8,32,1024]{2,1,0:T(8,128)(2,1)}, bf16[8,32,1024]{2,1,0:T(8,128)(2,1)S(1)}, u32[]{:S(2)}) copy-start(bf16[8,32,1024]{2,1,0:T(8,128)(2,1)S(1)} %collective-permute-done.3) | copy-start | bytes 1572868
  67.4 14.4 %collective-permute-start.5 = (bf16[8,32,1024]{2,1,0:T(8,128)(2,1)S(1)}, bf16[8,32,1024]{2,1,0:T(8,128)(2,1)S(1)}, u32[]{:S(2)}, u32[]{:S(2)}) collective-permute-start(bf16[8,32,1024]{2,1,0:T(8,128)(2,1)S(1)} %collective-permute-done.3), channel_id=1, source_target_pairs={{0,15},{1,0},{2,1},{3,2},{4,3},{5,4},{6,5},{7,6},{8,7},{9,8},{10,9... | collective-permute-start | bytes 1572872 | tf_op jit(solution)/shard_map/ppermute | solution.py:99
  81.7 13.5 %collective-permute-start.6 = (bf16[8,32,1024]{2,1,0:T(8,128)(2,1)S(1)}, bf16[8,32,1024]{2,1,0:T(8,128)(2,1)S(1)}, u32[]{:S(2)}, u32[]{:S(2)}) collective-permute-start(bf16[8,32,1024]{2,1,0:T(8,128)(2,1)S(1)} %collective-permute-done.4), channel_id=1, source_target_pairs={{0,1},{1,2},{2,3},{3,4},{4,5},{5,6},{6,7},{7,8},{8,9},{9,10},{10,1... | collective-permute-start | bytes 1572872 | tf_op jit(solution)/shard_map/ppermute | solution.py:94
  81.8 13.5 %collective-permute-start.7 = (bf16[8,32,1024]{2,1,0:T(8,128)(2,1)S(1)}, bf16[8,32,1024]{2,1,0:T(8,128)(2,1)S(1)}, u32[]{:S(2)}, u32[]{:S(2)}) collective-permute-start(bf16[8,32,1024]{2,1,0:T(8,128)(2,1)S(1)} %collective-permute-done.5), channel_id=1, source_target_pairs={{0,15},{1,0},{2,1},{3,2},{4,3},{5,4},{6,5},{7,6},{8,7},{9,8},{10,9... | collective-permute-start | bytes 1572872 | tf_op jit(solution)/shard_map/ppermute | solution.py:99
  95.3 12.7 %collective-permute-start.8 = (bf16[8,32,1024]{2,1,0:T(8,128)(2,1)S(1)}, bf16[8,32,1024]{2,1,0:T(8,128)(2,1)S(1)}, u32[]{:S(2)}, u32[]{:S(2)}) collective-permute-start(bf16[8,32,1024]{2,1,0:T(8,128)(2,1)S(1)} %collective-permute-done.6), channel_id=1, source_target_pairs={{0,1},{1,2},{2,3},{3,4},{4,5},{5,6},{6,7},{7,8},{8,9},{9,10},{10,1... | collective-permute-start | bytes 1572872 | tf_op jit(solution)/shard_map/ppermute | solution.py:94
  95.3 12.7 %collective-permute-start.9 = (bf16[8,32,1024]{2,1,0:T(8,128)(2,1)S(1)}, bf16[8,32,1024]{2,1,0:T(8,128)(2,1)}, u32[]{:S(2)}, u32[]{:S(2)}) collective-permute-start(bf16[8,32,1024]{2,1,0:T(8,128)(2,1)S(1)} %collective-permute-done.7), channel_id=1, source_target_pairs={{0,15},{1,0},{2,1},{3,2},{4,3},{5,4},{6,5},{7,6},{8,7},{9,8},{10,9... | collective-permute-start | bytes 1572872 | tf_op jit(solution)/shard_map/ppermute | solution.py:99
  108.0 11.9 %collective-permute-start.10 = (bf16[8,32,1024]{2,1,0:T(8,128)(2,1)S(1)}, bf16[8,32,1024]{2,1,0:T(8,128)(2,1)}, u32[]{:S(2)}, u32[]{:S(2)}) collective-permute-start(bf16[8,32,1024]{2,1,0:T(8,128)(2,1)S(1)} %collective-permute-done.8), channel_id=1, source_target_pairs={{0,1},{1,2},{2,3},{3,4},{4,5},{5,6},{6,7},{7,8},{8,9},{9,10},{10,1... | collective-permute-start | bytes 1572872 | tf_op jit(solution)/shard_map/ppermute | solution.py:94
  108.0 26.1 %collective-permute-start.11 = (bf16[8,32,1024]{2,1,0:T(8,128)(2,1)}, bf16[8,32,1024]{2,1,0:T(8,128)(2,1)}, u32[]{:S(2)}, u32[]{:S(2)}) collective-permute-start(bf16[8,32,1024]{2,1,0:T(8,128)(2,1)} %collective-permute-done.9), channel_id=1, source_target_pairs={{0,15},{1,0},{2,1},{3,2},{4,3},{5,4},{6,5},{7,6},{8,7},{9,8},{10,9... | collective-permute-start | bytes 1572872 | tf_op jit(solution)/shard_map/ppermute | solution.py:99
  120.0 18.9 %collective-permute-start.12 = (bf16[8,32,1024]{2,1,0:T(8,128)(2,1)}, bf16[8,32,1024]{2,1,0:T(8,128)(2,1)S(1)}, u32[]{:S(2)}, u32[]{:S(2)}) collective-permute-start(bf16[8,32,1024]{2,1,0:T(8,128)(2,1)} %collective-permute-done.10), channel_id=1, source_target_pairs={{0,1},{1,2},{2,3},{3,4},{4,5},{5,6},{6,7},{7,8},{8,9},{9,10},{10,1... | collective-permute-start | bytes 1572872 | tf_op jit(solution)/shard_map/ppermute | solution.py:94
  134.1 356.5 %collective-permute-start.13 = (bf16[8,32,1024]{2,1,0:T(8,128)(2,1)}, bf16[8,32,1024]{2,1,0:T(8,128)(2,1)}, u32[]{:S(2)}, u32[]{:S(2)}) collective-permute-start(bf16[8,32,1024]{2,1,0:T(8,128)(2,1)} %collective-permute-done.11), channel_id=1, source_target_pairs={{0,15},{1,0},{2,1},{3,2},{4,3},{5,4},{6,5},{7,6},{8,7},{9,8},{10,9... | collective-permute-start | bytes 1572872 | tf_op jit(solution)/shard_map/ppermute | solution.py:99
  138.9 378.1 %collective-permute-start.14 = (bf16[8,32,1024]{2,1,0:T(8,128)(2,1)S(1)}, bf16[8,32,1024]{2,1,0:T(8,128)(2,1)}, u32[]{:S(2)}, u32[]{:S(2)}) collective-permute-start(bf16[8,32,1024]{2,1,0:T(8,128)(2,1)S(1)} %collective-permute-done.12), channel_id=1, source_target_pairs={{0,1},{1,2},{2,3},{3,4},{4,5},{5,6},{6,7},{7,8},{8,9},{9,10},{10,1... | collective-permute-start | bytes 1572872 | tf_op jit(solution)/shard_map/ppermute | solution.py:94
  692.0 20.3 %all-to-all-start.1 = ((f32[8,32,1024]{2,1,0:T(8,128)}), f32[8,32,1024]{2,1,0:T(8,128)}, u32[]{:S(2)}, u32[]{:S(2)}) async-start(f32[8,32,1024]{2,1,0:T(8,128)} %broadcast_select_fusion), calls=%async_computation.2 | async-start | bytes 2097152 | tf_op jit(solution)/shard_map/all_to_all | solution.py:109
  (16 other events, 332.5 us)
Sparse Core Ops, SparseCore 0:
  571.9 117.0 reduce-scatter.1
